TPU v7x, 256 devices: a whole 4x4x8 slice. The times are simulated.
256 devices in a mesh: row: 32 (over z, y_hi, core), col: 8 (over x, y_lo).
Axes of the slice: x: 4, y: 4 (y_hi: 2, y_lo: 2; y = y_hi * 2 + y_lo), z: 8, core: 2. Of those that a mesh axis runs over, the one named last changes fastest.
Arguments:
- affinity_tiles: bfloat16 [1024, 512, 512], P(('row', 'col')), may hold values from -6 to 6
- tile_rows: int32 [1024], P(('row', 'col')), may hold values from -1 to 63, as said below
- tile_cols: int32 [1024], P(('row', 'col')), may hold values from -1 to 63, as said below
- lang_counts: int32 [32], replicated, may hold values from 1 to 8192, 32768 in all
- start_basis: float32 [8, 4096, 64], P('col', 'row'), may hold values from -6 to 6
Outputs:
- eigen_basis: float32 [8, 4096, 64], P('col', 'row')
Inputs may be any that keep to these rules, and one draw needn't show every extreme that they name: `tile_rows`: the slots of device (r, c) are entries (r * 8 + c) * 4 onward of both lists. Every used slot names a distinct block with block row from r * 2 to (r + 1) * 2 - 1, block column from c * 8 to (c + 1) * 8 - 1, and block row <= block column; no block is named twice. Empty slots hold -1 in both lists and come after the used slots of their device. Device (0, 7) uses all 4 slots. `tile_cols`: same slots as tile_rows.
All inputs are finite; a program needn't handle non-finite values.
Results may differ from a plain program's by a relative error of at most 0.0044.
Values may be sent and summed in bfloat16 or wider, within the bound.
No kernel may reach another device: no remote copies, remote signals or barrier semaphores. Data moves between devices by JAX's collectives and lax.ppermute only.
A program may use at most 64 MiB of HBM per device.

v0:
```python
import jax
import jax.numpy as jnp
from jax import lax
from jax.sharding import PartitionSpec as P

ROW_BLOCKS = 2
ITERS = 3
highest = lax.Precision.HIGHEST


def broadcast(value, axis, root):
    mine = lax.axis_index(axis) == root
    return lax.psum(jnp.where(mine, value, jnp.zeros_like(value)), axis)


def add_block(target, addend, offset):
    current = lax.dynamic_slice_in_dim(target, offset, addend.shape[0], 0)
    return lax.dynamic_update_slice_in_dim(target, current + addend, offset, 0)


def membership(first_doc, doc_count, lang_ends, lang_starts):
    doc_index = first_doc + jnp.arange(doc_count, dtype=jnp.int32)
    return (
        (doc_index[:, None] >= lang_starts[None, :]) & (doc_index[:, None] < lang_ends[None, :])
    ).astype(jnp.float32)


def apply_tiles(affinity_tiles, pick_rows, pick_cols, scaled_rows, scaled_cols, col_blocks):
    slot_count, tile_size, _ = affinity_tiles.shape
    vectors = scaled_cols.shape[1]
    blocks_r = scaled_rows.reshape(ROW_BLOCKS, tile_size, vectors)
    blocks_c = scaled_cols.reshape(col_blocks, tile_size, vectors)
    chosen_c = jnp.einsum(
        "tq,qjk->tjk", pick_cols, blocks_c, preferred_element_type=jnp.float32
    ).astype(jnp.bfloat16)
    chosen_r = jnp.einsum(
        "tp,pik->tik", pick_rows, blocks_r, preferred_element_type=jnp.float32
    ).astype(jnp.bfloat16)
    forward = jnp.einsum(
        "tij,tjk->tik", affinity_tiles, chosen_c, preferred_element_type=jnp.float32
    )
    backward = jnp.einsum(
        "tij,tik->tjk", affinity_tiles, chosen_r, preferred_element_type=jnp.float32
    )
    part_rows = jnp.einsum("tp,tik->pik", pick_rows.astype(jnp.float32), forward, precision=highest)
    part_cols = jnp.einsum(
        "tq,tjk->qjk", pick_cols.astype(jnp.float32), backward, precision=highest
    )
    return (
        part_rows.reshape(ROW_BLOCKS * tile_size, vectors),
        part_cols.reshape(col_blocks * tile_size, vectors),
    )


def shards(affinity_tiles, tile_rows, tile_cols, lang_counts, start_basis):
    row_devices = lax.axis_size("row")
    col_devices = lax.axis_size("col")
    group_ratio = row_devices // col_devices
    col_blocks = ROW_BLOCKS * row_devices // col_devices
    tile_size = affinity_tiles.shape[1]
    row_span = ROW_BLOCKS * tile_size
    col_span = col_blocks * tile_size
    piece_rows = start_basis.shape[1]
    doc_total = piece_rows * row_devices * col_devices
    my_row = lax.axis_index("row")
    my_col = lax.axis_index("col")
    is_owner = (my_row // group_ratio == my_col).astype(jnp.float32)
    offset = my_row % group_ratio * row_span
    piece_offset = my_row * piece_rows
    present = tile_rows >= 0
    local_p = tile_rows - my_row * ROW_BLOCKS
    local_q = tile_cols - my_col * col_blocks
    pick_rows = (
        (local_p[:, None] == jnp.arange(ROW_BLOCKS, dtype=jnp.int32)[None, :]) & present[:, None]
    ).astype(jnp.bfloat16)
    pick_cols = (
        (local_q[:, None] == jnp.arange(col_blocks, dtype=jnp.int32)[None, :]) & present[:, None]
    ).astype(jnp.bfloat16)
    magnitude = jnp.abs(affinity_tiles)
    row_mass = jnp.sum(magnitude, axis=2, dtype=jnp.float32)
    col_mass = jnp.sum(magnitude, axis=1, dtype=jnp.float32)
    degree_rows = jnp.einsum(
        "tp,ti->pi", pick_rows.astype(jnp.float32), row_mass, precision=highest
    ).reshape(row_span)
    degree_cols = jnp.einsum(
        "tq,tj->qj", pick_cols.astype(jnp.float32), col_mass, precision=highest
    ).reshape(col_span)
    rows_degree = lax.psum(degree_rows, "col")
    degree_cols = add_block(degree_cols, is_owner * rows_degree, offset)
    inv_own = lax.rsqrt(1.0 + lax.psum_scatter(degree_cols, "row", scatter_dimension=0, tiled=True))
    prior_scale = lax.psum(jnp.sum(inv_own), ("row", "col")) / doc_total
    lang_ends = jnp.cumsum(lang_counts)
    lang_starts = lang_ends - lang_counts
    counts_real = lang_counts.astype(jnp.float32)
    member_own = membership(my_col * col_span + piece_offset, piece_rows, lang_ends, lang_starts)
    basis_own = start_basis[0]
    for iteration in range(ITERS):
        lang_now = lax.psum(jnp.dot(member_own.T, basis_own, precision=highest), ("row", "col"))
        lang_mean = prior_scale * (lang_now / counts_real[:, None])
        scaled_cols = lax.all_gather(
            (inv_own[:, None] * basis_own).astype(jnp.bfloat16), "row", axis=0, tiled=True
        )
        scaled_rows = broadcast(
            lax.dynamic_slice_in_dim(scaled_cols, offset, row_span, 0), "col", my_row // group_ratio
        )
        part_rows, part_cols = apply_tiles(
            affinity_tiles, pick_rows, pick_cols, scaled_rows, scaled_cols, col_blocks
        )
        rows_sum = lax.psum(part_rows, "col")
        part_cols = add_block(part_cols, is_owner * rows_sum, offset)
        product_own = lax.psum_scatter(part_cols, "row", scatter_dimension=0, tiled=True)
        applied_own = inv_own[:, None] * product_own + jnp.dot(
            member_own, lang_mean, precision=highest
        )
        gram_part = jnp.dot(applied_own.T, applied_own, precision=highest)
        gram_matrix = lax.psum(gram_part, ("row", "col"))
        factor = jnp.linalg.cholesky(gram_matrix / doc_total)
        basis_own = jax.scipy.linalg.solve_triangular(factor, applied_own.T, lower=True).T
    return basis_own[None]


def solution(mesh):
    in_specs = (
        P(("row", "col"), None, None),
        P(("row", "col")),
        P(("row", "col")),
        P(),
        P("col", "row", None),
    )
    out_specs = P("col", "row", None)
    return jax.shard_map(shards, mesh=mesh, in_specs=in_specs, out_specs=out_specs, check_vma=False)
```

profile of v0, /device:TPU:1, one launch (start us, length us, event | category | flops | bytes accessed | tf_op | source)
XLA Modules:
  0.0 1385.8 jit_solution(9308302912916534671)
XLA Ops:
  6.5 0.7 broadcast_compare_fusion
  7.2 0.7 broadcast_subtract_fusion
  7.9 0.7 broadcast_subtract_fusion.1
  8.6 2.2 convert_reduce_fusion
  11.0 16.9 %psum.98 = f32[1024]{0:T(1024)S(1)} all-reduce(f32[1024]{0:T(1024)S(1)} %bitcast.181), channel_id=1, replica_groups=mesh['row'=32,'col'=8] {'col'}, use_global_device_ids=true, to_apply=%region_2.3 | all-reduce | flops 1024 | bytes 8192 | tf_op jit(solution)/shard_map/psum | solution.py:88
  28.1 130.8 %all-reduce = f32[4096]{0:T(1024)S(1)} all-reduce(f32[4096]{0:T(1024)S(1)} %add_dynamic-update-slice_fusion.3), channel_id=2, replica_groups=mesh['row'=32,'col'=8] {'row'}, use_global_device_ids=true, to_apply=%region_3.4.clone | all-reduce | flops 4096 | bytes 32768
  160.2 0.7 fusion.72
  160.8 43.6 %all_gather.9 = bf16[4096,64]{0,1:T(8,128)(2,1)S(1)} all-gather(bf16[128,64]{0,1:T(8,128)(2,1)S(1)} %fusion.39), channel_id=1, replica_groups=mesh['row'=32,'col'=8] {'row'}, dimensions={0}, use_global_device_ids=true | all-gather | bytes 540672 | tf_op jit(solution)/shard_map/all_gather | solution.py:100
  204.5 0.7 reshape.85
  205.7 0.7 convolution_bitcast_fusion.4
  206.5 0.9 fusion.8
  207.4 0.7 copy.46
  208.2 67.3 %all-reduce.9.cloned.1.call-done = bf16[2,512,64]{1,0,2:T(2,128)(2,1)} async-done(((bf16[2,512,64]{1,0,2:T(2,128)(2,1)}), bf16[2,512,64]{1,0,2:T(2,128)(2,1)}) %all-reduce.9.cloned.1.call-update) | async-done | bytes 131088 | tf_op jit(solution)/shard_map/psum | solution.py:13
  275.5 1.2 convolution_convert_fusion.5
  277.2 1.0 fusion.10
  278.9 77.9 %all-reduce.11.cloned.1.call-done = f32[1024,64]{0,1:T(8,128)} async-done(((f32[1024,64]{0,1:T(8,128)}), f32[1024,64]{0,1:T(8,128)}) %all-reduce.11.cloned.1.call-update) | async-done | bytes 262160 | tf_op jit(solution)/shard_map/psum | solution.py:109
  356.7 1.0 add_dynamic-update-slice_fusion.2
  357.7 1.0 copy-done.2
  359.3 79.9 %all-reduce.1 = (f32[32,64]{1,0:T(8,128)S(1)}, f32[]{:T(128)}) all-reduce(f32[32,64]{1,0:T(8,128)S(1)} %fusion.22, f32[]{:T(128)} %get-tuple-element.11), channel_id=1, replica_groups=mesh['row'=32,'col'=8] {'row','col'}, use_global_device_ids=true, to_apply=%region_10.11 | all-reduce | flops 2049 | bytes 16392 | tf_op jit(solution)/shard_map/psum | solution.py:98
  439.9 36.3 %reduce-scatter.4.cloned.1.call-done = f32[128,64]{0,1:T(8,128)} async-done(((f32[4096,64]{0,1:T(8,128)}), f32[128,64]{0,1:T(8,128)}) %reduce-scatter.4.cloned.1.call-update) | async-done | bytes 32784 | tf_op jit(solution)/shard_map/reduce_scatter | solution.py:111
  476.2 1.1 convolution_add_fusion.2
  477.4 79.7 %psum.103 = f32[64,64]{0,1:T(8,128)S(1)} all-reduce(f32[64,64]{0,1:T(8,128)S(1)} %fusion.75), channel_id=1, replica_groups=mesh['row'=32,'col'=8] {'row','col'}, use_global_device_ids=true, to_apply=%region_11.12 | all-reduce | flops 4096 | bytes 32768 | tf_op jit(solution)/shard_map/psum | solution.py:116
  557.2 5.8 cholesky.59
  563.1 0.6 compare_reduce_fusion.2
  563.8 0.7 fusion.24
  564.4 4.9 custom-call.7
  569.6 41.2 %all_gather.10 = bf16[4096,64]{0,1:T(8,128)(2,1)S(1)} all-gather(bf16[128,64]{0,1:T(8,128)(2,1)S(1)} %fusion.44), channel_id=1, replica_groups=mesh['row'=32,'col'=8] {'row'}, dimensions={0}, use_global_device_ids=true | all-gather | bytes 540672 | tf_op jit(solution)/shard_map/all_gather | solution.py:100
  610.8 0.7 reshape.91
  612.2 0.7 convolution_bitcast_fusion.2
  613.0 0.9 fusion.4
  613.9 0.7 copy.49
  614.7 65.5 %all-reduce.13.cloned.1.call-done = bf16[2,512,64]{1,0,2:T(2,128)(2,1)} async-done(((bf16[2,512,64]{1,0,2:T(2,128)(2,1)}), bf16[2,512,64]{1,0,2:T(2,128)(2,1)}) %all-reduce.13.cloned.1.call-update) | async-done | bytes 131088 | tf_op jit(solution)/shard_map/psum | solution.py:13
  680.2 1.2 convolution_convert_fusion.4
  681.9 1.0 fusion.6
  683.5 77.7 %all-reduce.15.cloned.1.call-done = f32[1024,64]{0,1:T(8,128)} async-done(((f32[1024,64]{0,1:T(8,128)}), f32[1024,64]{0,1:T(8,128)}) %all-reduce.15.cloned.1.call-update) | async-done | bytes 262160 | tf_op jit(solution)/shard_map/psum | solution.py:109
  761.2 1.0 add_dynamic-update-slice_fusion.1
  762.2 1.0 copy-done.3
  763.5 79.8 %psum.106 = f32[32,64]{1,0:T(8,128)S(1)} all-reduce(f32[32,64]{1,0:T(8,128)S(1)} %fusion.20), channel_id=1, replica_groups=mesh['row'=32,'col'=8] {'row','col'}, use_global_device_ids=true, to_apply=%region_17.20 | all-reduce | flops 2048 | bytes 16384 | tf_op jit(solution)/shard_map/psum | solution.py:98
  843.3 37.3 %reduce-scatter.6.cloned.1.call-done = f32[128,64]{0,1:T(8,128)} async-done(((f32[4096,64]{0,1:T(8,128)}), f32[128,64]{0,1:T(8,128)}) %reduce-scatter.6.cloned.1.call-update) | async-done | bytes 32784 | tf_op jit(solution)/shard_map/reduce_scatter | solution.py:111
  880.5 1.1 convolution_add_fusion.1
  881.8 79.7 %psum.107 = f32[64,64]{0,1:T(8,128)S(1)} all-reduce(f32[64,64]{0,1:T(8,128)S(1)} %fusion.76), channel_id=1, replica_groups=mesh['row'=32,'col'=8] {'row','col'}, use_global_device_ids=true, to_apply=%region_18.21 | all-reduce | flops 4096 | bytes 32768 | tf_op jit(solution)/shard_map/psum | solution.py:116
  961.6 5.8 cholesky.70
  967.5 0.6 compare_reduce_fusion.1
  968.1 0.7 fusion.25
  968.8 4.9 custom-call.8
  974.0 41.2 %all_gather.11 = bf16[4096,64]{0,1:T(8,128)(2,1)S(1)} all-gather(bf16[128,64]{0,1:T(8,128)(2,1)S(1)} %fusion.45), channel_id=1, replica_groups=mesh['row'=32,'col'=8] {'row'}, dimensions={0}, use_global_device_ids=true | all-gather | bytes 540672 | tf_op jit(solution)/shard_map/all_gather | solution.py:100
  1015.2 0.7 reshape.95
  1016.4 0.7 convolution_bitcast_fusion
  1017.2 0.9 fusion
  1018.1 0.7 copy.52
  1019.1 65.4 %all-reduce.17.cloned.1.call-done = bf16[2,512,64]{1,0,2:T(2,128)(2,1)} async-done(((bf16[2,512,64]{1,0,2:T(2,128)(2,1)}), bf16[2,512,64]{1,0,2:T(2,128)(2,1)}) %all-reduce.17.cloned.1.call-update) | async-done | bytes 131088 | tf_op jit(solution)/shard_map/psum | solution.py:13
  1084.6 1.2 convolution_convert_fusion.3
  1086.3 1.0 fusion.2
  1087.9 77.9 %all-reduce.19.cloned.1.call-done = f32[1024,64]{0,1:T(8,128)} async-done(((f32[1024,64]{0,1:T(8,128)}), f32[1024,64]{0,1:T(8,128)}) %all-reduce.19.cloned.1.call-update) | async-done | bytes 262160 | tf_op jit(solution)/shard_map/psum | solution.py:109
  1165.7 1.0 add_dynamic-update-slice_fusion
  1166.8 1.0 copy-done.1
  1168.0 79.8 %psum.110 = f32[32,64]{1,0:T(8,128)S(1)} all-reduce(f32[32,64]{1,0:T(8,128)S(1)} %fusion.18), channel_id=1, replica_groups=mesh['row'=32,'col'=8] {'row','col'}, use_global_device_ids=true, to_apply=%region_22.25 | all-reduce | flops 2048 | bytes 16384 | tf_op jit(solution)/shard_map/psum | solution.py:98
  1247.8 37.4 %reduce-scatter.8.cloned.1.call-done = f32[128,64]{0,1:T(8,128)} async-done(((f32[4096,64]{0,1:T(8,128)}), f32[128,64]{0,1:T(8,128)}) %reduce-scatter.8.cloned.1.call-update) | async-done | bytes 32784 | tf_op jit(solution)/shard_map/reduce_scatter | solution.py:111
  1285.2 1.1 convolution_add_fusion
  1286.5 79.7 %psum.111 = f32[64,64]{0,1:T(8,128)S(1)} all-reduce(f32[64,64]{0,1:T(8,128)S(1)} %fusion.77), channel_id=1, replica_groups=mesh['row'=32,'col'=8] {'row','col'}, use_global_device_ids=true, to_apply=%region_23.26 | all-reduce | flops 4096 | bytes 32768 | tf_op jit(solution)/shard_map/psum | solution.py:116
  1366.3 5.8 cholesky.81
  1372.8 0.7 fusion.26
  1373.5 4.9 custom-call.9
  1378.4 0.9 convolution_bitcast_fusion.6
  (81 shorter events, 9.6 us)
Async XLA Ops:
  6.5 152.4 %copy-start.6 = (u32[256]{0:T(256)S(1)}, u32[256]{0:T(256)}, u32[]{:S(2)}) copy-start(u32[256]{0:T(256)} %constant.105) | copy-start | bytes 3076
  6.5 154.3 %copy-start.4 = (f32[1,128,64]{1,2,0:T(8,128)S(1)}, f32[1,128,64]{1,2,0:T(8,128)}, u32[]{:S(2)}) copy-start(f32[1,128,64]{1,2,0:T(8,128)} %param.12) | copy-start | bytes 98308
  6.5 269.0 %all-reduce.9.cloned.1.call-start = ((), (), s32[]{:S(2)}) async-start(), calls=%async_computation.3 | async-start | bytes 262144 | tf_op jit(solution)/shard_map/psum | solution.py:13
  10.8 194.9 %copy-start = (bf16[4,512,512]{2,1,0:T(8,128)(2,1)S(1)}, bf16[4,512,512]{2,1,0:T(8,128)(2,1)}, u32[]{:S(2)}) copy-start(bf16[4,512,512]{2,1,0:T(8,128)(2,1)} %param.8) | copy-start | bytes 6291460
  205.2 151.5 %all-reduce.11.cloned.1.call-start = ((), (), s32[]{:S(2)}) async-start(), calls=%async_computation.4 | async-start | bytes 524288 | tf_op jit(solution)/shard_map/psum | solution.py:109
  208.2 268.0 %reduce-scatter.4.cloned.1.call-start = ((), (), s32[]{:S(2)}) async-start(), calls=%async_computation.5 | async-start | bytes 1081344 | tf_op jit(solution)/shard_map/reduce_scatter | solution.py:111
  278.2 80.6 %copy-start.5 = (s32[32]{0:T(128)S(1)}, s32[32]{0:T(128)}, u32[]{:S(2)}) copy-start(s32[32]{0:T(128)} %param.11) | copy-start | bytes 388
  357.7 1.0 copy-start.2
  358.7 321.4 %all-reduce.13.cloned.1.call-start = ((), (), s32[]{:S(2)}) async-start(), calls=%async_computation.6 | async-start | bytes 262144 | tf_op jit(solution)/shard_map/psum | solution.py:13
  611.5 149.7 %all-reduce.15.cloned.1.call-start = ((), (), s32[]{:S(2)}) async-start(), calls=%async_computation.7 | async-start | bytes 524288 | tf_op jit(solution)/shard_map/psum | solution.py:109
  614.6 265.9 %reduce-scatter.6.cloned.1.call-start = ((), (), s32[]{:S(2)}) async-start(), calls=%async_computation.8 | async-start | bytes 1081344 | tf_op jit(solution)/shard_map/reduce_scatter | solution.py:111
  762.2 1.0 copy-start.3
  763.2 321.3 %all-reduce.17.cloned.1.call-start = ((), (), s32[]{:S(2)}) async-start(), calls=%async_computation.9 | async-start | bytes 262144 | tf_op jit(solution)/shard_map/psum | solution.py:13
  1015.9 149.9 %all-reduce.19.cloned.1.call-start = ((), (), s32[]{:S(2)}) async-start(), calls=%async_computation.10 | async-start | bytes 524288 | tf_op jit(solution)/shard_map/psum | solution.py:109
  1018.8 266.4 %reduce-scatter.8.cloned.1.call-start = ((), (), s32[]{:S(2)}) async-start(), calls=%async_computation.11 | async-start | bytes 1081344 | tf_op jit(solution)/shard_map/reduce_scatter | solution.py:111
  1166.8 1.0 copy-start.1
Sparse Core Ops, SparseCore 0:
  205.3 70.1 all-reduce.8
  278.1 78.5 all-reduce.10
  360.8 115.3 reduce-scatter.3
  611.6 68.4 all-reduce.12
  682.6 78.5 all-reduce.14
  765.1 115.3 reduce-scatter.5
  1016.0 68.5 all-reduce.16
  1087.2 78.5 all-reduce.18
  1169.8 115.3 reduce-scatter.7
where the time goes:
time: 1390 us
  blocking collectives  752 us (54%)
  waiting for transfers between devices  543 us (39%)
  other arithmetic  44.5 us (3%)
  matrix products  20 us (1%)
  between operations  15 us (1%)
    psum x3, blocking collectives, shards(): lax.psum(jnp.dot(member_own.T, basis_own, precision=highest), ('row', 'co...  239 us
    psum x3, blocking collectives, shards(): gram_matrix = lax.psum(gram_part, ('row', 'col'))  239 us
    psum x3, waiting for transfers between devices, shards(): rows_sum = lax.psum(part_rows, 'col')  233 us
    psum x3, waiting for transfers between devices, broadcast(): return lax.psum(jnp.where(mine, value, jnp.zeros_like(value)), axis)  198 us
    unnamed x1, blocking collectives  131 us
    all_gather x3, blocking collectives, shards(): lax.all_gather((inv_own[:, None] * basis_own).astype(jnp.bfloat16), 'row'...  126 us
    reduce_scatter x3, waiting for transfers between devices, shards(): lax.psum_scatter(part_cols, 'row', scatter_dimension=0, tiled=True)  111 us
  transfers between devices with their start and end apart: 9, of which 9 were waited for; matrix products, arithmetic and copies ran while one was open for 1% of the time, Pallas kernels for 0%

commit v1 on v0

--- a/solution.py
+++ b/solution.py
@@ -97,8 +97,16 @@
     for iteration in range(ITERS):
         lang_now = lax.psum(jnp.dot(member_own.T, basis_own, precision=highest), ("row", "col"))
         lang_mean = prior_scale * (lang_now / counts_real[:, None])
-        scaled_cols = lax.all_gather(
-            (inv_own[:, None] * basis_own).astype(jnp.bfloat16), "row", axis=0, tiled=True
+        scaled_cols = jnp.concatenate(
+            lax.all_to_all(
+                jnp.stack(
+                    [(inv_own[:, None] * basis_own).astype(jnp.bfloat16)] * lax.axis_size("row")
+                ),
+                "row",
+                0,
+                0,
+            ),
+            axis=0,
         )
         scaled_rows = broadcast(
             lax.dynamic_slice_in_dim(scaled_cols, offset, row_span, 0), "col", my_row // group_ratio

time: 1390 us -> 1340 us (0.964)
  blocking collectives: 752 us -> 674 us
  waiting for transfers between devices: 543 us -> 559 us
    all_gather x3 -> x0, blocking collectives: 126 us -> none  [shards(): lax.all_gather((inv_own[:, None] * basis_own).astype(jnp.bfloat16), 'row'...]
    all_to_all x0 -> x2, blocking collectives: none -> 47.5 us  [shards(): lax.all_to_all(jnp.stack([(inv_own[:, None] * basis_own).astype(jnp.bfloa...]
    all_to_all x0 -> x1, waiting for transfers between devices: none -> 16.8 us  [shards(): lax.all_to_all(jnp.stack([(inv_own[:, None] * basis_own).astype(jnp.bfloa...]
  transfers between devices with their start and end apart: 9 -> 10, of which waited for: 9 -> 10; matrix products, arithmetic and copies ran while one was open for 1% -> 1% of each run, Pallas kernels for 0% -> 0%
where the time goes in v1:
time: 1340 us
  blocking collectives  674 us (50%)
  waiting for transfers between devices  559 us (42%)
  other arithmetic  44.5 us (3%)
  matrix products  19.9 us (1%)
  between operations  15 us (1%)
  local copies, waits for them, and re-layouts  13.4 us (1%)
    psum x3, blocking collectives, shards(): lax.psum(jnp.dot(member_own.T, basis_own, precision=highest), ('row', 'co...  239 us
    psum x3, blocking collectives, shards(): gram_matrix = lax.psum(gram_part, ('row', 'col'))  239 us
    psum x3, waiting for transfers between devices, shards(): rows_sum = lax.psum(part_rows, 'col')  234 us
    psum x3, waiting for transfers between devices, broadcast(): return lax.psum(jnp.where(mine, value, jnp.zeros_like(value)), axis)  198 us
    unnamed x1, blocking collectives  131 us
    reduce_scatter x3, waiting for transfers between devices, shards(): lax.psum_scatter(part_cols, 'row', scatter_dimension=0, tiled=True)  111 us
    all_to_all x2, blocking collectives, shards(): lax.all_to_all(jnp.stack([(inv_own[:, None] * basis_own).astype(jnp.bfloa...  47.5 us
  transfers between devices with their start and end apart: 10, of which 10 were waited for; matrix products, arithmetic and copies ran while one was open for 1% of the time, Pallas kernels for 0%

profile of v1, /device:TPU:1, one launch (start us, length us, event | category | flops | bytes accessed | tf_op | source)
XLA Modules:
  0.0 1337.2 jit_solution(12234896880980572750)
XLA Ops:
  6.5 0.7 broadcast_compare_fusion
  7.2 0.7 broadcast_subtract_fusion
  7.9 0.7 broadcast_subtract_fusion.1
  8.6 2.2 convert_reduce_fusion
  11.0 16.8 %psum.98 = f32[1024]{0:T(1024)S(1)} all-reduce(f32[1024]{0:T(1024)S(1)} %bitcast.183), channel_id=1, replica_groups=mesh['row'=32,'col'=8] {'col'}, use_global_device_ids=true, to_apply=%region_2.3 | all-reduce | flops 1024 | bytes 8192 | tf_op jit(solution)/shard_map/psum | solution.py:88
  28.0 130.8 %all-reduce = f32[4096]{0:T(1024)S(1)} all-reduce(f32[4096]{0:T(1024)S(1)} %add_dynamic-update-slice_fusion.3), channel_id=2, replica_groups=mesh['row'=32,'col'=8] {'row'}, use_global_device_ids=true, to_apply=%region_3.4.clone | all-reduce | flops 4096 | bytes 32768
  160.0 0.7 fusion.72
  160.7 0.9 stack.9
  161.6 10.8 all-to-all-start
  172.5 16.8 %all-to-all-done = bf16[32,128,64]{1,2,0:T(8,128)(2,1)S(1)} async-done(((bf16[32,128,64]{1,2,0:T(8,128)(2,1)}), bf16[32,128,64]{1,2,0:T(8,128)(2,1)S(1)}, u32[]{:S(2)}, u32[]{:S(2)}) %all-to-all-start) | async-done | bytes 524320 | tf_op jit(solution)/shard_map/all_to_all | solution.py:101
  189.4 0.7 reshape.95
  191.1 0.7 convolution_bitcast_fusion.4
  191.9 0.9 fusion.8
  192.8 0.7 copy.82
  193.6 65.7 %all-reduce.9.cloned.1.call-done = bf16[2,512,64]{1,0,2:T(2,128)(2,1)} async-done(((bf16[2,512,64]{1,0,2:T(2,128)(2,1)}), bf16[2,512,64]{1,0,2:T(2,128)(2,1)}) %all-reduce.9.cloned.1.call-update) | async-done | bytes 131088 | tf_op jit(solution)/shard_map/psum | solution.py:13
  259.3 1.2 convolution_convert_fusion.5
  261.0 1.0 fusion.10
  262.6 77.9 %all-reduce.11.cloned.1.call-done = f32[1024,64]{0,1:T(8,128)} async-done(((f32[1024,64]{0,1:T(8,128)}), f32[1024,64]{0,1:T(8,128)}) %all-reduce.11.cloned.1.call-update) | async-done | bytes 262160 | tf_op jit(solution)/shard_map/psum | solution.py:117
  340.5 1.0 add_dynamic-update-slice_fusion.2
  341.5 1.0 copy-done.2
  343.1 79.9 %all-reduce.1 = (f32[32,64]{1,0:T(8,128)S(1)}, f32[]{:T(128)}) all-reduce(f32[32,64]{1,0:T(8,128)S(1)} %fusion.22, f32[]{:T(128)} %get-tuple-element.11), channel_id=1, replica_groups=mesh['row'=32,'col'=8] {'row','col'}, use_global_device_ids=true, to_apply=%region_10.11 | all-reduce | flops 2049 | bytes 16392 | tf_op jit(solution)/shard_map/psum | solution.py:98
  423.6 36.3 %reduce-scatter.4.cloned.1.call-done = f32[128,64]{0,1:T(8,128)} async-done(((f32[4096,64]{0,1:T(8,128)}), f32[128,64]{0,1:T(8,128)}) %reduce-scatter.4.cloned.1.call-update) | async-done | bytes 32784 | tf_op jit(solution)/shard_map/reduce_scatter | solution.py:119
  459.9 1.1 convolution_add_fusion.2
  461.2 79.7 %psum.103 = f32[64,64]{0,1:T(8,128)S(1)} all-reduce(f32[64,64]{0,1:T(8,128)S(1)} %fusion.75), channel_id=1, replica_groups=mesh['row'=32,'col'=8] {'row','col'}, use_global_device_ids=true, to_apply=%region_11.12 | all-reduce | flops 4096 | bytes 32768 | tf_op jit(solution)/shard_map/psum | solution.py:124
  541.0 5.8 cholesky.59
  547.5 0.7 fusion.24
  548.2 4.9 custom-call.7
  553.4 23.8 %all_to_all.15 = bf16[32,128,64]{1,2,0:T(8,128)(2,1)S(1)} all-to-all(bf16[32,128,64]{1,2,0:T(8,128)(2,1)S(1)} %stack.10), channel_id=1, replica_groups=mesh['row'=32,'col'=8] {'row'}, dimensions={0} | all-to-all | bytes 1048576 | tf_op jit(solution)/shard_map/all_to_all | solution.py:101
  577.3 0.7 reshape.101
  579.1 0.7 convolution_bitcast_fusion.2
  579.8 0.9 fusion.4
  580.7 0.7 copy.84
  581.5 66.3 %all-reduce.13.cloned.1.call-done = bf16[2,512,64]{1,0,2:T(2,128)(2,1)} async-done(((bf16[2,512,64]{1,0,2:T(2,128)(2,1)}), bf16[2,512,64]{1,0,2:T(2,128)(2,1)}) %all-reduce.13.cloned.1.call-update) | async-done | bytes 131088 | tf_op jit(solution)/shard_map/psum | solution.py:13
  647.8 1.2 convolution_convert_fusion.4
  649.5 1.0 fusion.6
  651.1 77.7 %all-reduce.15.cloned.1.call-done = f32[1024,64]{0,1:T(8,128)} async-done(((f32[1024,64]{0,1:T(8,128)}), f32[1024,64]{0,1:T(8,128)}) %all-reduce.15.cloned.1.call-update) | async-done | bytes 262160 | tf_op jit(solution)/shard_map/psum | solution.py:117
  728.8 1.0 add_dynamic-update-slice_fusion.1
  729.8 1.0 copy-done.3
  731.1 79.8 %psum.106 = f32[32,64]{1,0:T(8,128)S(1)} all-reduce(f32[32,64]{1,0:T(8,128)S(1)} %fusion.20), channel_id=1, replica_groups=mesh['row'=32,'col'=8] {'row','col'}, use_global_device_ids=true, to_apply=%region_17.20 | all-reduce | flops 2048 | bytes 16384 | tf_op jit(solution)/shard_map/psum | solution.py:98
  810.9 37.2 %reduce-scatter.6.cloned.1.call-done = f32[128,64]{0,1:T(8,128)} async-done(((f32[4096,64]{0,1:T(8,128)}), f32[128,64]{0,1:T(8,128)}) %reduce-scatter.6.cloned.1.call-update) | async-done | bytes 32784 | tf_op jit(solution)/shard_map/reduce_scatter | solution.py:119
  848.1 1.1 convolution_add_fusion.1
  849.4 79.7 %psum.107 = f32[64,64]{0,1:T(8,128)S(1)} all-reduce(f32[64,64]{0,1:T(8,128)S(1)} %fusion.76), channel_id=1, replica_groups=mesh['row'=32,'col'=8] {'row','col'}, use_global_device_ids=true, to_apply=%region_18.21 | all-reduce | flops 4096 | bytes 32768 | tf_op jit(solution)/shard_map/psum | solution.py:124
  929.2 5.8 cholesky.70
  935.7 0.7 fusion.25
  936.4 4.9 custom-call.8
  941.7 23.7 %all_to_all.16 = bf16[32,128,64]{1,2,0:T(8,128)(2,1)S(1)} all-to-all(bf16[32,128,64]{1,2,0:T(8,128)(2,1)S(1)} %stack.11), channel_id=1, replica_groups=mesh['row'=32,'col'=8] {'row'}, dimensions={0} | all-to-all | bytes 1048576 | tf_op jit(solution)/shard_map/all_to_all | solution.py:101
  965.5 0.7 reshape.105
  967.3 0.7 convolution_bitcast_fusion
  968.0 0.9 fusion
  968.9 0.7 copy.86
  970.0 66.1 %all-reduce.17.cloned.1.call-done = bf16[2,512,64]{1,0,2:T(2,128)(2,1)} async-done(((bf16[2,512,64]{1,0,2:T(2,128)(2,1)}), bf16[2,512,64]{1,0,2:T(2,128)(2,1)}) %all-reduce.17.cloned.1.call-update) | async-done | bytes 131088 | tf_op jit(solution)/shard_map/psum | solution.py:13
  1036.0 1.2 convolution_convert_fusion.3
  1037.7 1.0 fusion.2
  1039.3 77.9 %all-reduce.19.cloned.1.call-done = f32[1024,64]{0,1:T(8,128)} async-done(((f32[1024,64]{0,1:T(8,128)}), f32[1024,64]{0,1:T(8,128)}) %all-reduce.19.cloned.1.call-update) | async-done | bytes 262160 | tf_op jit(solution)/shard_map/psum | solution.py:117
  1117.2 1.0 add_dynamic-update-slice_fusion
  1118.2 1.0 copy-done.1
  1119.5 79.8 %psum.110 = f32[32,64]{1,0:T(8,128)S(1)} all-reduce(f32[32,64]{1,0:T(8,128)S(1)} %fusion.18), channel_id=1, replica_groups=mesh['row'=32,'col'=8] {'row','col'}, use_global_device_ids=true, to_apply=%region_22.25 | all-reduce | flops 2048 | bytes 16384 | tf_op jit(solution)/shard_map/psum | solution.py:98
  1199.3 37.4 %reduce-scatter.8.cloned.1.call-done = f32[128,64]{0,1:T(8,128)} async-done(((f32[4096,64]{0,1:T(8,128)}), f32[128,64]{0,1:T(8,128)}) %reduce-scatter.8.cloned.1.call-update) | async-done | bytes 32784 | tf_op jit(solution)/shard_map/reduce_scatter | solution.py:119
  1236.7 1.1 convolution_add_fusion
  1238.0 79.7 %psum.111 = f32[64,64]{0,1:T(8,128)S(1)} all-reduce(f32[64,64]{0,1:T(8,128)S(1)} %fusion.77), channel_id=1, replica_groups=mesh['row'=32,'col'=8] {'row','col'}, use_global_device_ids=true, to_apply=%region_23.26 | all-reduce | flops 4096 | bytes 32768 | tf_op jit(solution)/shard_map/psum | solution.py:124
  1317.8 5.8 cholesky.81
  1324.3 0.7 fusion.26
  1324.9 4.9 custom-call.9
  1329.8 0.9 convolution_bitcast_fusion.6
  (91 shorter events, 12.6 us)
Async XLA Ops:
  6.5 152.2 %copy-start.6 = (u32[256]{0:T(256)S(1)}, u32[256]{0:T(256)}, u32[]{:S(2)}) copy-start(u32[256]{0:T(256)} %constant.105) | copy-start | bytes 3076
  6.5 154.2 %copy-start.4 = (f32[1,128,64]{1,2,0:T(8,128)S(1)}, f32[1,128,64]{1,2,0:T(8,128)}, u32[]{:S(2)}) copy-start(f32[1,128,64]{1,2,0:T(8,128)} %param.12) | copy-start | bytes 98308
  161.6 27.6 %all-to-all-start = ((bf16[32,128,64]{1,2,0:T(8,128)(2,1)}), bf16[32,128,64]{1,2,0:T(8,128)(2,1)S(1)}, u32[]{:S(2)}, u32[]{:S(2)}) async-start(bf16[32,128,64]{1,2,0:T(8,128)(2,1)} %stack.9), calls=%async_computation | async-start | bytes 1048576 | tf_op jit(solution)/shard_map/all_to_all | solution.py:101
  172.4 86.9 %all-reduce.9.cloned.1.call-start = ((), (), s32[]{:S(2)}) async-start(), calls=%async_computation.6 | async-start | bytes 262144 | tf_op jit(solution)/shard_map/psum | solution.py:13
  172.4 18.7 %copy-start = (bf16[4,512,512]{2,1,0:T(8,128)(2,1)S(1)}, bf16[4,512,512]{2,1,0:T(8,128)(2,1)}, u32[]{:S(2)}) copy-start(bf16[4,512,512]{2,1,0:T(8,128)(2,1)} %param.8) | copy-start | bytes 6291460
  191.1 149.4 %all-reduce.11.cloned.1.call-start = ((), (), s32[]{:S(2)}) async-start(), calls=%async_computation.7 | async-start | bytes 524288 | tf_op jit(solution)/shard_map/psum | solution.py:117
  193.5 266.4 %reduce-scatter.4.cloned.1.call-start = ((), (), s32[]{:S(2)}) async-start(), calls=%async_computation.8 | async-start | bytes 1081344 | tf_op jit(solution)/shard_map/reduce_scatter | solution.py:119
  262.0 80.6 %copy-start.5 = (s32[32]{0:T(128)S(1)}, s32[32]{0:T(128)}, u32[]{:S(2)}) copy-start(s32[32]{0:T(128)} %param.11) | copy-start | bytes 388
  341.5 1.0 copy-start.2
  342.5 305.3 %all-reduce.13.cloned.1.call-start = ((), (), s32[]{:S(2)}) async-start(), calls=%async_computation.9 | async-start | bytes 262144 | tf_op jit(solution)/shard_map/psum | solution.py:13
  579.0 149.8 %all-reduce.15.cloned.1.call-start = ((), (), s32[]{:S(2)}) async-start(), calls=%async_computation.10 | async-start | bytes 524288 | tf_op jit(solution)/shard_map/psum | solution.py:117
  581.5 266.6 %reduce-scatter.6.cloned.1.call-start = ((), (), s32[]{:S(2)}) async-start(), calls=%async_computation.11 | async-start | bytes 1081344 | tf_op jit(solution)/shard_map/reduce_scatter | solution.py:119
  729.8 1.0 copy-start.3
  730.9 305.2 %all-reduce.17.cloned.1.call-start = ((), (), s32[]{:S(2)}) async-start(), calls=%async_computation.12 | async-start | bytes 262144 | tf_op jit(solution)/shard_map/psum | solution.py:13
  967.2 150.0 %all-reduce.19.cloned.1.call-start = ((), (), s32[]{:S(2)}) async-start(), calls=%async_computation.13 | async-start | bytes 524288 | tf_op jit(solution)/shard_map/psum | solution.py:117
  969.7 267.0 %reduce-scatter.8.cloned.1.call-start = ((), (), s32[]{:S(2)}) async-start(), calls=%async_computation.14 | async-start | bytes 1081344 | tf_op jit(solution)/shard_map/reduce_scatter | solution.py:119
  1118.2 1.0 copy-start.1
Sparse Core Ops, SparseCore 0:
  191.2 68.0 all-reduce.8
  261.9 78.5 all-reduce.10
  344.6 115.3 reduce-scatter.3
  579.1 68.6 all-reduce.12
  650.3 78.5 all-reduce.14
  732.8 115.3 reduce-scatter.5
  967.3 68.6 all-reduce.16
  1038.6 78.5 all-reduce.18
  1121.3 115.3 reduce-scatter.7
